TPU v7x, 128 devices: a whole 4x4x4 slice. The times are simulated.
128 devices in a mesh: pix: 8 (over y_hi, z), tm: 16 (over x, y_lo, core).
Axes of the slice: x: 4, y: 4 (y_hi: 2, y_lo: 2; y = y_hi * 2 + y_lo), z: 4, core: 2. Of those that a mesh axis runs over, the one named last changes fastest.
Arguments:
- frames: float32 [16, 192, 12288], P('tm', 'pix'), may hold values from 0.05 to 5
- pixel_order: int32 [12288], replicated, may hold values from 0 to 12287, each once
- cycle_sizes: int32 [64], replicated, may hold values from 1 to 384, 12288 in all
- kernel: float32 [5], replicated, may hold values from 0.1 to 1
Outputs:
- correlation: float32 [64, 3072, 3072], P('pix', 'tm')
Inputs may be any that keep to these rules, and one draw needn't show every extreme that they name: `cycle_sizes`: every cycle has one or more pixels, the sizes sum to 12288, and one cycle has exactly 384.
All inputs are finite; a program needn't handle non-finite values.
Results may differ from a plain program's by a relative error of at most 0.00005.
Values sent between devices are 32-bit elements; how exact they have to be, the bound alone decides.
No kernel may reach another device: no remote copies, remote signals or barrier semaphores. Data moves between devices by JAX's collectives and lax.ppermute only.
A program may use at most 256 MiB of HBM per device.

v0:
```python
import jax
import jax.numpy as jnp
from jax import lax
from jax.sharding import PartitionSpec as P

REACH = 2


def halo_frames(block, width):
    count = lax.axis_size("tm")
    forward = [(i, i + 1) for i in range(count - 1)]
    backward = [(i + 1, i) for i in range(count - 1)]
    n = block.shape[-1]
    low = lax.ppermute(block[..., n - width :], "tm", forward)
    high = lax.ppermute(block[..., :width], "tm", backward)
    return jnp.concatenate([low, block, high], axis=-1)


def correlate(left, right):
    return jnp.einsum(
        "rfs,rgs->rfg",
        left,
        right,
        precision=lax.Precision.HIGH,
        preferred_element_type=jnp.float32,
    )


def per_device(frames, pixel_order, cycle_sizes, kernel):
    block = frames[0]
    sub, pixels = block.shape
    cycles = cycle_sizes.shape[0]
    cap = 2 * pixels // cycles
    groups = lax.axis_size("pix")
    owned = cycles // groups
    counts = [owned - owned * 5 // 8, owned * 5 // 8]
    firsts = [sum(counts[:i]) for i in range(len(counts))]
    tblk = groups * sub
    starts = (jnp.cumsum(cycle_sizes) - cycle_sizes).astype(jnp.int32).reshape(groups, owned)
    me = lax.axis_index("pix")
    mine = lax.dynamic_index_in_dim(starts, me, 0, keepdims=False)
    sizes = lax.dynamic_index_in_dim(cycle_sizes.reshape(groups, owned), me, 0, keepdims=False)
    slots = jnp.arange(cap, dtype=jnp.int32)
    lanes = 32
    longest = max(counts) * cap + lanes
    count = pixels // lanes + longest // lanes
    order = (
        jnp.pad(pixel_order, (0, count * lanes - pixels)).reshape(count, lanes).astype(jnp.float32)
    )
    series = block.T
    outs = []
    for part, (step, first) in enumerate(zip(counts, firsts)):
        span = step * cap + lanes
        aligned = starts[:, first] // lanes * lanes
        rows = (aligned // lanes)[:, None] + jnp.arange(span // lanes, dtype=jnp.int32)
        pick_rows = (rows[..., None] == jnp.arange(count, dtype=jnp.int32)).astype(jnp.float32)
        window = jnp.einsum(
            "drk,kl->drl",
            pick_rows,
            order,
            precision=lax.Precision.HIGHEST,
            preferred_element_type=jnp.float32,
        )
        window = window.astype(jnp.int32).reshape(groups * span)
        chunks = series.at[window].get(mode="promise_in_bounds").reshape(groups, span, sub)
        got = lax.all_to_all(chunks, "pix", 0, 0, tiled=True)
        got = jnp.pad(got, ((0, 0), (0, cap), (0, 0)))
        offsets = mine[first : first + step] - mine[first] // lanes * lanes
        masks = slots[None, :] < sizes[first : first + step, None]
        picked = []
        for l in range(step):
            taken = lax.dynamic_slice_in_dim(got, offsets[l], cap, 1)
            picked.append(jnp.where(masks[l][None, :, None], taken, 0.0))
        picked = jnp.stack(picked)
        picked = jnp.transpose(picked, (0, 2, 1, 3)).reshape(step, cap, tblk)
        total = jnp.sum(picked, axis=1, keepdims=True)
        scaled = picked / total
        scale = sizes[first : first + step].astype(jnp.float32)[:, None, None]
        if part == 0:
            whole = lax.all_gather(jnp.swapaxes(scaled, 1, 2), "tm", axis=1, tiled=True)
            frames_all = whole.shape[1]
            rimmed = jnp.pad(whole, ((0, 0), (REACH, REACH), (0, 0)))
            right = kernel[0] * rimmed[:, 0:frames_all]
            for shift_step in range(1, 2 * REACH + 1):
                right = right + kernel[shift_step] * rimmed[:, shift_step : shift_step + frames_all]
            smooth = lax.dynamic_slice_in_dim(right, lax.axis_index("tm") * tblk, tblk, 1)
        else:
            rimmed = halo_frames(scaled, REACH)
            smooth = kernel[0] * rimmed[..., 0:tblk]
            for shift_step in range(1, 2 * REACH + 1):
                smooth = smooth + kernel[shift_step] * rimmed[..., shift_step : shift_step + tblk]
            smooth = jnp.swapaxes(smooth, 1, 2)
            right = lax.all_gather(smooth, "tm", axis=1, tiled=True)
        outs.append(correlate(smooth * scale, right))
    last = counts[-1]
    result = lax.optimization_barrier(
        jnp.pad(jnp.concatenate(outs[:-1], 0), ((0, last), (0, 0), (0, 0)))
    )
    return lax.dynamic_update_slice_in_dim(result, outs[-1], owned - last, 0)


def solution(mesh):
    placed = (P("tm", "pix", None), P(), P(), P())
    return jax.shard_map(
        per_device, mesh=mesh, in_specs=placed, out_specs=P("pix", "tm", None), check_vma=False
    )
```

profile of v0, /device:TPU:1, one launch (start us, length us, event | category | flops | bytes accessed | tf_op | source)
XLA Modules:
  0.0 314.3 jit_solution(2399621395003718831)
XLA Ops:
  6.5 0.8 copy.10
  7.6 0.7 sub.37
  8.3 0.2 fusion.52
  8.6 0.8 pad_convert_fusion
  9.5 0.8 convolution_convert_fusion.1
  10.8 4.0 %copy.9 = f32[1,24,12288]{1,2,0:T(8,128)} copy(f32[1,24,12288]{2,1,0:T(8,128)S(1)} %copy-done.1) | data formatting | bytes 2359296 | tf_op args[0]
  14.8 21.1 %gather_fusion = f32[9472,24]{1,0:T(8,128)} fusion(f32[12288,24]{1,0:T(8,128)} %bitcast.76, s32[10240]{0:T(1024)S(1)} %pad_clamp_fusion.1), kind=kCustom, calls=%fused_computation | custom fusion | bytes 1856512 | tf_op jit(solution)/shard_map/gather | solution.py:65
  35.8 3.9 %copy.13 = f32[8,1184,24]{1,2,0:T(8,128)} copy(f32[8,1184,24]{2,1,0:T(8,128)} %bitcast.79) | data formatting | bytes 1818624 | tf_op jit(solution)/shard_map/reshape | solution.py:65
  39.8 8.6 %all-to-all-start = ((f32[8,1184,24]{1,2,0:T(8,128)}), f32[8,1184,24]{1,2,0:T(8,128)S(1)}, u32[]{:S(2)}, u32[]{:S(2)}) async-start(f32[8,1184,24]{1,2,0:T(8,128)} %copy.13), calls=%async_computation | async-start | bytes 1966080 | tf_op jit(solution)/shard_map/all_to_all | solution.py:66
  48.5 0.6 fusion.62
  51.7 0.7 fusion.64
  58.3 3.6 %all-to-all-done = f32[8,1184,24]{1,2,0:T(8,128)S(1)} async-done(((f32[8,1184,24]{1,2,0:T(8,128)}), f32[8,1184,24]{1,2,0:T(8,128)S(1)}, u32[]{:S(2)}, u32[]{:S(2)}) %all-to-all-start) | async-done | bytes 909344 | tf_op jit(solution)/shard_map/all_to_all | solution.py:66
  61.9 0.3 fusion.21
  62.5 1.1 bitcast_divide_fusion.1
  63.7 0.9 convolution_convert_fusion
  65.2 32.3 %gather_fusion.1 = f32[15616,24]{1,0:T(8,128)} fusion(f32[12288,24]{1,0:T(8,128)} %bitcast.77, s32[16384]{0:T(1024)S(1)} %pad_clamp_fusion), kind=kCustom, calls=%fused_computation.1 | custom fusion | bytes 3060736 | tf_op jit(solution)/shard_map/gather | solution.py:65
  97.5 6.1 %copy.16 = f32[8,1952,24]{1,2,0:T(8,128)} copy(f32[8,1952,24]{2,1,0:T(8,128)} %bitcast.78) | data formatting | bytes 2998272 | tf_op jit(solution)/shard_map/reshape | solution.py:65
  103.6 5.9 %all-to-all-start.1 = ((f32[8,1952,24]{1,2,0:T(8,128)}), f32[8,1952,24]{1,2,0:T(8,128)S(1)}, u32[]{:S(2)}, u32[]{:S(2)}) async-start(f32[8,1952,24]{1,2,0:T(8,128)} %copy.16), calls=%async_computation.1 | async-start | bytes 3145728 | tf_op jit(solution)/shard_map/all_to_all | solution.py:66
  112.1 0.6 fusion.61
  122.0 25.3 %all-to-all-done.1 = f32[8,1952,24]{1,2,0:T(8,128)S(1)} async-done(((f32[8,1952,24]{1,2,0:T(8,128)}), f32[8,1952,24]{1,2,0:T(8,128)S(1)}, u32[]{:S(2)}, u32[]{:S(2)}) %all-to-all-start.1) | async-done | bytes 1499168 | tf_op jit(solution)/shard_map/all_to_all | solution.py:66
  148.1 0.2 bitcast_reduce_fusion
  148.4 0.2 bitcast_divide_fusion
  148.7 3.8 %collective-permute-start = (f32[5,384,2]{1,2,0:T(2,128)S(1)}, f32[5,384,2]{1,2,0:T(2,128)S(1)}, u32[]{:S(2)}, u32[]{:S(2)}) collective-permute-start(f32[5,384,2]{1,2,0:T(2,128)S(1)} %get-tuple-element.15), channel_id=1, source_target_pairs={{0,1},{1,2},{2,3},{3,4},{4,5},{5,6},{6,7},{7,8},{8,9},{9,10},{10,1... | collective-permute-start | bytes 46088 | tf_op jit(solution)/shard_map/ppermute | solution.py:14
  152.5 2.1 collective-permute-start.1
  154.6 0.7 fusion.63
  155.3 3.1 collective-permute-done.1
  158.4 5.0 %fusion.5 = f32[5,192,384]{2,1,0:T(8,128)} fusion(f32[5,384,192]{1,2,0:T(8,128)S(1)} %bitcast_divide_fusion, f32[5,384,2]{1,2,0:T(2,128)S(1)} %collective-permute-done.1, f32[5,384,2]{1,2,0:T(2,128)S(1)} %collective-permute-done, f32[]{:T(128)} %bitcast.20, f32[]{:T(128)} %bitcast.19, f32[]{:T(128)} %bitcast.18, f32[]{:T(128)} %bitcast.17, f32[]{:T(128)} %bitcast), kind=kLoop, calls=%fused_computation.19 | loop fusion | flops 4792320 | bytes 2979860 | tf_op jit(solution)/shard_map/transpose | solution.py:92
  163.5 33.8 %multiply_add_fusion = f32[3,3072,384]{2,1,0:T(8,128)} fusion(f32[3,3072,384]{2,1,0:T(8,128)} %all-gather.3.cloned.1.call-done, f32[]{:T(128)} %bitcast.20, f32[]{:T(128)} %bitcast.19, f32[]{:T(128)} %bitcast.18, f32[]{:T(128)} %bitcast.17, f32[]{:T(128)} %bitcast), kind=kLoop, calls=%fused_computation.2 | loop fusion | flops 31850496 | bytes 28311572 | tf_op jit(solution)/shard_map/add | solution.py:85
  197.3 13.4 %fusion.13 = f32[3,192,3072]{2,1,0:T(8,128)} fusion(f32[3,3072,384]{2,1,0:T(8,128)} %multiply_add_fusion, s32[]{:T(128)S(6)} %select_n.119, f32[3]{0:T(128)S(1)} %get-tuple-element.29), kind=kOutput, calls=%fused_computation.40 | convolution fusion | flops 4077084672 | bytes 22118416 | tf_op jit(solution)/shard_map/rfs,rgs->rfg/dot_general | solution.py:20
  210.7 12.7 %pad.23 = f32[8,192,3072]{2,1,0:T(8,128)} pad(f32[3,192,3072]{2,1,0:T(8,128)} %fusion.13, f32[]{:T(128)} %constant.86.clone.1), padding=0_5x0_0x0_0 | pad | bytes 25952260 | tf_op jit(solution)/shard_map/jit(_pad)/pad | solution.py:97
  223.5 63.8 %all-gather.5.cloned.1.call-done = f32[5,3072,384]{2,1,0:T(8,128)} async-done(((f32[5,192,384]{2,1,0:T(8,128)}), f32[5,3072,384]{2,1,0:T(8,128)}) %all-gather.5.cloned.1.call-update) | async-done | bytes 23592976 | tf_op jit(solution)/shard_map/all_gather | solution.py:93
  287.2 20.2 %convolution_dynamic-update-slice_fusion = f32[8,192,3072]{2,1,0:T(8,128)} fusion(f32[8,192,3072]{2,1,0:T(8,128)} %pad.23, f32[5,3072,384]{2,1,0:T(8,128)} %all-gather.5.cloned.1.call-done, f32[5,192,384]{2,1,0:T(8,128)S(1)} %copy-done, f32[5]{0:T(128)S(1)} %get-tuple-element.20), kind=kOutput, calls=%fused_computation.5 | convolution fusion | flops 6795141120 | bytes 36864020 | tf_op jit(solution)/shard_map/rfs,rgs->rfg/dot_general | solution.py:20
  (48 shorter events, 3.2 us)
Async XLA Ops:
  6.5 4.2 %copy-start.1 = (f32[1,24,12288]{2,1,0:T(8,128)S(1)}, f32[1,24,12288]{2,1,0:T(8,128)}, u32[]{:S(2)}) copy-start(f32[1,24,12288]{2,1,0:T(8,128)} %param.4) | copy-start | bytes 3538948
  39.8 8.7 %copy-start.3 = (s32[64]{0:T(128)S(1)}, s32[64]{0:T(128)}, u32[]{:S(2)}) copy-start(s32[64]{0:T(128)} %param.6) | copy-start | bytes 772
  39.8 22.1 %all-to-all-start = ((f32[8,1184,24]{1,2,0:T(8,128)}), f32[8,1184,24]{1,2,0:T(8,128)S(1)}, u32[]{:S(2)}, u32[]{:S(2)}) async-start(f32[8,1184,24]{1,2,0:T(8,128)} %copy.13), calls=%async_computation | async-start | bytes 1966080 | tf_op jit(solution)/shard_map/all_to_all | solution.py:66
  48.4 115.1 %all-gather.3.cloned.1.call-start = ((), (), s32[]{:S(2)}) async-start(), calls=%async_computation.2 | async-start | bytes 15040512 | tf_op jit(solution)/shard_map/all_gather | solution.py:80
  103.6 43.8 %all-to-all-start.1 = ((f32[8,1952,24]{1,2,0:T(8,128)}), f32[8,1952,24]{1,2,0:T(8,128)S(1)}, u32[]{:S(2)}, u32[]{:S(2)}) async-start(f32[8,1952,24]{1,2,0:T(8,128)} %copy.16), calls=%async_computation.1 | async-start | bytes 3145728 | tf_op jit(solution)/shard_map/all_to_all | solution.py:66
  109.5 177.7 %all-gather.5.cloned.1.call-start = ((), (), s32[]{:S(2)}) async-start(), calls=%async_computation.3 | async-start | bytes 25067520 | tf_op jit(solution)/shard_map/all_gather | solution.py:93
  148.4 6.2 %copy-start.2 = (f32[5]{0:T(128)S(1)}, f32[5]{0:T(128)}, u32[]{:S(2)}) copy-start(f32[5]{0:T(128)} %param.7) | copy-start | bytes 64
  148.7 6.6 %collective-permute-start = (f32[5,384,2]{1,2,0:T(2,128)S(1)}, f32[5,384,2]{1,2,0:T(2,128)S(1)}, u32[]{:S(2)}, u32[]{:S(2)}) collective-permute-start(f32[5,384,2]{1,2,0:T(2,128)S(1)} %get-tuple-element.15), channel_id=1, source_target_pairs={{0,1},{1,2},{2,3},{3,4},{4,5},{5,6},{6,7},{7,8},{8,9},{9,10},{10,1... | collective-permute-start | bytes 46088 | tf_op jit(solution)/shard_map/ppermute | solution.py:14
  152.5 5.9 %collective-permute-start.1 = (f32[5,384,2]{1,2,0:T(2,128)S(1)}, f32[5,384,2]{1,2,0:T(2,128)S(1)}, u32[]{:S(2)}, u32[]{:S(2)}) collective-permute-start(f32[5,384,2]{1,2,0:T(2,128)S(1)} %get-tuple-element.16), channel_id=1, source_target_pairs={{1,0},{2,1},{3,2},{4,3},{5,4},{6,5},{7,6},{8,7},{9,8},{10,9},{11,1... | collective-permute-start | bytes 46088 | tf_op jit(solution)/shard_map/ppermute | solution.py:15
  210.7 76.5 %copy-start = (f32[5,192,384]{2,1,0:T(8,128)S(1)}, f32[5,192,384]{2,1,0:T(8,128)}, u32[]{:S(2)}) copy-start(f32[5,192,384]{2,1,0:T(8,128)} %fusion.5) | copy-start | bytes 4423684
Sparse Core Ops, SparseCore 0:
  63.7 97.0 all-gather.2
  163.6 123.6 all-gather.4
where the time goes:
time: 315 us; the launch traced here: 314 us
  waiting for transfers between devices  95.8 us (30%)
  local copies, waits for them, and re-layouts  84.6 us (27%)
  other arithmetic  44.3 us (14%)
  matrix products  35.4 us (11%)
  between operations  33.7 us (11%)
  starting transfers between devices  20.5 us (7%)
    all_gather x1, waiting for transfers between devices, per_device(): right = lax.all_gather(smooth, 'tm', axis=1, tiled=True)  63.8 us
    gather x2, local copies, waits for them, and re-layouts, per_device(): series.at[window].get(mode='promise_in_bounds').reshape(groups, span, sub)  53.4 us
    add x1, other arithmetic, per_device(): right + kernel[shift_step] * rimmed[:, shift_step:shift_step + frames_all]  33.8 us
    dot_general x2, matrix products, correlate(): jnp.einsum('rfs,rgs->rfg', left, right, precision=lax.Precision.HIGH, pre...  33.6 us
    all_to_all x2, waiting for transfers between devices, per_device(): got = lax.all_to_all(chunks, 'pix', 0, 0, tiled=True)  28.9 us
    all_to_all x2, starting transfers between devices, per_device(): got = lax.all_to_all(chunks, 'pix', 0, 0, tiled=True)  14.5 us
    pad x1, local copies, waits for them, and re-layouts, per_device(): jnp.pad(jnp.concatenate(outs[:-1], 0), ((0, last), (0, 0), (0, 0)))  12.7 us
    reshape x2, local copies, waits for them, and re-layouts, per_device(): series.at[window].get(mode='promise_in_bounds').reshape(groups, span, sub)  10 us
  transfers between devices with their start and end apart: 6, of which 4 were waited for; matrix products, arithmetic and copies ran while one was open for 35% of the time, Pallas kernels for 0%

commit v1 on v0

--- a/solution.py
+++ b/solution.py
@@ -90,7 +90,8 @@
             for shift_step in range(1, 2 * REACH + 1):
                 smooth = smooth + kernel[shift_step] * rimmed[..., shift_step : shift_step + tblk]
             smooth = jnp.swapaxes(smooth, 1, 2)
-            right = lax.all_gather(smooth, "tm", axis=1, tiled=True)
+            sent = jnp.stack([smooth] * lax.axis_size("tm"))
+            right = jnp.concatenate(lax.all_to_all(sent, "tm", 0, 0), axis=1)
         outs.append(correlate(smooth * scale, right))
     last = counts[-1]
     result = lax.optimization_barrier(

time: 315 us -> 667 us (2.12)
  waiting for transfers between devices: 95.8 us -> 416 us
  local copies, waits for them, and re-layouts: 84.6 us -> 113 us
    all_to_all x0 -> x1, waiting for transfers between devices: none -> 384 us  [per_device(): right = jnp.concatenate(lax.all_to_all(sent, 'tm', 0, 0), axis=1)]
    all_gather x1 -> x0, waiting for transfers between devices: 63.8 us -> none  [per_device(): right = lax.all_gather(smooth, 'tm', axis=1, tiled=True)]
    reshape x0 -> x1, local copies, waits for them, and re-layouts: none -> 16.7 us  [per_device(): right = jnp.concatenate(lax.all_to_all(sent, 'tm', 0, 0), axis=1)]
    another operation x1 -> x2, local copies, waits for them, and re-layouts: 0.84 us -> 11.4 us  [the longest x1 10.7 us: per_device(): sent = jnp.stack([smooth] * lax.axis_size('tm'))]
  transfers between devices with their start and end apart: 6 -> 6, of which waited for: 4 -> 4; matrix products, arithmetic and copies ran while one was open for 35% -> 11% of each run, Pallas kernels for 0% -> 0%
where the time goes in v1:
time: 667 us; the launch traced here: 666 us
  waiting for transfers between devices  416 us (62%)
  local copies, waits for them, and re-layouts  113 us (17%)
  other arithmetic  41.6 us (6%)
  matrix products  35.2 us (5%)
  between operations  34 us (5%)
  starting transfers between devices  26.1 us (4%)
    all_to_all x1, waiting for transfers between devices, per_device(): right = jnp.concatenate(lax.all_to_all(sent, 'tm', 0, 0), axis=1)  384 us
    gather x2, local copies, waits for them, and re-layouts, per_device(): series.at[window].get(mode='promise_in_bounds').reshape(groups, span, sub)  53.4 us
    dot_general x2, matrix products, correlate(): jnp.einsum('rfs,rgs->rfg', left, right, precision=lax.Precision.HIGH, pre...  33.4 us
    add x1, other arithmetic, per_device(): right + kernel[shift_step] * rimmed[:, shift_step:shift_step + frames_all]  32.3 us
    all_to_all x2, waiting for transfers between devices, per_device(): got = lax.all_to_all(chunks, 'pix', 0, 0, tiled=True)  28.5 us
    reshape x1, local copies, waits for them, and re-layouts, per_device(): right = jnp.concatenate(lax.all_to_all(sent, 'tm', 0, 0), axis=1)  16.7 us
    all_to_all x2, starting transfers between devices, per_device(): got = lax.all_to_all(chunks, 'pix', 0, 0, tiled=True)  14.5 us
  transfers between devices with their start and end apart: 6, of which 4 were waited for; matrix products, arithmetic and copies ran while one was open for 11% of the time, Pallas kernels for 0%

profile of v1, /device:TPU:1, one launch (start us, length us, event | category | flops | bytes accessed | tf_op | source)
XLA Modules:
  0.0 665.7 jit_solution(715000178404263284)
XLA Ops:
  6.5 0.7 copy.18
  7.5 0.7 sub.37
  8.4 0.8 pad_convert_fusion
  9.4 4.9 copy.17
  14.3 0.8 convolution_convert_fusion.1
  15.6 21.1 %gather_fusion = f32[9472,24]{1,0:T(8,128)} fusion(f32[12288,24]{1,0:T(8,128)} %bitcast.78, s32[10240]{0:T(1024)S(1)} %pad_clamp_fusion.1), kind=kCustom, calls=%fused_computation | custom fusion | bytes 1856512 | tf_op jit(solution)/shard_map/gather | solution.py:65
  36.6 3.9 copy.21
  40.6 8.6 %all-to-all-start = ((f32[8,1184,24]{1,2,0:T(8,128)}), f32[8,1184,24]{1,2,0:T(8,128)S(1)}, u32[]{:S(2)}, u32[]{:S(2)}) async-start(f32[8,1184,24]{1,2,0:T(8,128)} %copy.21), calls=%async_computation | async-start | bytes 1966080 | tf_op jit(solution)/shard_map/all_to_all | solution.py:66
  49.3 0.7 fusion.62
  52.6 0.7 fusion.64
  59.2 3.5 all-to-all-done
  62.7 0.3 fusion.21
  63.3 1.1 bitcast_divide_fusion.1
  64.5 0.9 convolution_convert_fusion
  66.0 32.3 %gather_fusion.1 = f32[15616,24]{1,0:T(8,128)} fusion(f32[12288,24]{1,0:T(8,128)} %bitcast.79, s32[16384]{0:T(1024)S(1)} %pad_clamp_fusion), kind=kCustom, calls=%fused_computation.1 | custom fusion | bytes 3060736 | tf_op jit(solution)/shard_map/gather | solution.py:65
  98.3 6.1 copy.24
  104.4 5.9 all-to-all-start.1
  112.9 0.7 fusion.61
  123.2 24.9 %all-to-all-done.1 = f32[8,1952,24]{1,2,0:T(8,128)S(1)} async-done(((f32[8,1952,24]{1,2,0:T(8,128)}), f32[8,1952,24]{1,2,0:T(8,128)S(1)}, u32[]{:S(2)}, u32[]{:S(2)}) %all-to-all-start.1) | async-done | bytes 1499168 | tf_op jit(solution)/shard_map/all_to_all | solution.py:66
  149.5 3.8 collective-permute-start
  153.3 1.9 collective-permute-start.1
  155.2 0.7 fusion.63
  155.9 3.3 collective-permute-done.1
  159.2 3.9 fusion.5
  163.1 10.7 %stack.59 = f32[16,5,192,384]{3,2,1,0:T(8,128)} broadcast(f32[5,192,384]{2,1,0:T(8,128)S(1)} %fusion.5), dimensions={1,2,3} | broadcast | bytes 25067520 | tf_op jit(solution)/shard_map/stack | solution.py:93
  173.8 5.9 all-to-all-start.2
  179.7 384.3 %all-to-all-done.2 = f32[16,5,192,384]{3,2,1,0:T(8,128)} async-done(((f32[16,5,192,384]{3,2,1,0:T(8,128)}), f32[16,5,192,384]{3,2,1,0:T(8,128)}, u32[]{:S(2)}, u32[]{:S(2)}) %all-to-all-start.2) | async-done | bytes 23592992 | tf_op jit(solution)/shard_map/all_to_all | solution.py:94
  564.0 16.7 %copy.25 = f32[5,16,192,384]{3,2,1,0:T(8,128)} copy(f32[5,16,192,384]{3,2,0,1:T(8,128)} %bitcast.39) | data formatting | bytes 47185920 | tf_op jit(solution)/shard_map/reshape | solution.py:94
  580.7 32.3 %multiply_add_fusion = f32[3,3072,384]{2,1,0:T(8,128)} fusion(f32[3,3072,384]{2,1,0:T(8,128)} %all-gather.2.cloned.1.call-done, f32[]{:T(128)} %bitcast.20, f32[]{:T(128)} %bitcast.19, f32[]{:T(128)} %bitcast.18, f32[]{:T(128)} %bitcast.17, f32[]{:T(128)} %bitcast), kind=kLoop, calls=%fused_computation.2 | loop fusion | flops 31850496 | bytes 28311572 | tf_op jit(solution)/shard_map/add | solution.py:85
  612.9 13.2 %fusion.13 = f32[3,192,3072]{2,1,0:T(8,128)} fusion(f32[3,3072,384]{2,1,0:T(8,128)} %multiply_add_fusion, s32[]{:T(128)S(6)} %select_n.119, f32[3]{0:T(128)S(1)} %get-tuple-element.29), kind=kOutput, calls=%fused_computation.40 | convolution fusion | flops 4077084672 | bytes 22118416 | tf_op jit(solution)/shard_map/rfs,rgs->rfg/dot_general | solution.py:20
  626.2 12.5 %pad.23 = f32[8,192,3072]{2,1,0:T(8,128)} pad(f32[3,192,3072]{2,1,0:T(8,128)} %fusion.13, f32[]{:T(128)} %constant.86.clone.1), padding=0_5x0_0x0_0 | pad | bytes 25952260 | tf_op jit(solution)/shard_map/jit(_pad)/pad | solution.py:98
  638.7 20.2 %convolution_dynamic-update-slice_fusion = f32[8,192,3072]{2,1,0:T(8,128)} fusion(f32[8,192,3072]{2,1,0:T(8,128)} %pad.23, f32[5,3072,384]{2,1,0:T(8,128)} %bitcast.80, f32[5,192,384]{2,1,0:T(8,128)S(1)} %fusion.5, f32[5]{0:T(128)S(1)} %get-tuple-element.20), kind=kOutput, calls=%fused_computation.5 | convolution fusion | flops 6795141120 | bytes 36864020 | tf_op jit(solution)/shard_map/rfs,rgs->rfg/dot_general | solution.py:20
  (45 shorter events, 3.7 us)
Async XLA Ops:
  40.6 8.7 %copy-start.1 = (s32[64]{0:T(128)S(1)}, s32[64]{0:T(128)}, u32[]{:S(2)}) copy-start(s32[64]{0:T(128)} %param.6) | copy-start | bytes 772
  40.6 22.1 %all-to-all-start = ((f32[8,1184,24]{1,2,0:T(8,128)}), f32[8,1184,24]{1,2,0:T(8,128)S(1)}, u32[]{:S(2)}, u32[]{:S(2)}) async-start(f32[8,1184,24]{1,2,0:T(8,128)} %copy.21), calls=%async_computation | async-start | bytes 1966080 | tf_op jit(solution)/shard_map/all_to_all | solution.py:66
  49.2 531.5 %all-gather.2.cloned.1.call-start = ((), (), s32[]{:S(2)}) async-start(), calls=%async_computation.3 | async-start | bytes 15040512 | tf_op jit(solution)/shard_map/all_gather | solution.py:80
  104.4 43.8 %all-to-all-start.1 = ((f32[8,1952,24]{1,2,0:T(8,128)}), f32[8,1952,24]{1,2,0:T(8,128)S(1)}, u32[]{:S(2)}, u32[]{:S(2)}) async-start(f32[8,1952,24]{1,2,0:T(8,128)} %copy.24), calls=%async_computation.1 | async-start | bytes 3145728 | tf_op jit(solution)/shard_map/all_to_all | solution.py:66
  149.2 6.1 copy-start
  149.5 6.4 collective-permute-start
  153.3 5.9 collective-permute-start.1
  173.8 390.1 %all-to-all-start.2 = ((f32[16,5,192,384]{3,2,1,0:T(8,128)}), f32[16,5,192,384]{3,2,1,0:T(8,128)}, u32[]{:S(2)}, u32[]{:S(2)}) async-start(f32[16,5,192,384]{3,2,1,0:T(8,128)} %stack.59), calls=%async_computation.2 | async-start | bytes 47185920 | tf_op jit(solution)/shard_map/all_to_all | solution.py:94
Sparse Core Ops, SparseCore 0:
  64.6 97.0 all-gather.1
